TPU v7x, 512 devices: a whole 4x4x16 slice. The times are simulated.
512 devices in a mesh: fibre: 128 (over x, y_hi, z), seg: 4 (over y_lo, core).
Axes of the slice: x: 4, y: 4 (y_hi: 2, y_lo: 2; y = y_hi * 2 + y_lo), z: 16, core: 2. Of those that a mesh axis runs over, the one named last changes fastest.
Arguments:
- data: bfloat16 [4, 1024, 2048], P('seg', 'fibre')
- sources: int32 [2, 4], replicated, may hold values from 0 to 7
- owners: int32 [2], replicated, may hold values from 0 to 127
Outputs:
- correlations: float32 [2, 4, 1024, 1024], P(None, None, ('fibre', 'seg'))
All inputs are finite; a program needn't handle non-finite values.
Results may differ from a plain program's by a relative error of at most 0.0066.
Values may be sent and summed in bfloat16 or wider, within the bound.
No kernel may reach another device: no remote copies, remote signals or barrier semaphores. Data moves between devices by JAX's collectives and lax.ppermute only.
A program may use at most 64 MiB of HBM per device.

v0:
```python
import math
import jax
import jax.numpy as jnp
from jax import lax
from jax.sharding import PartitionSpec as P

BAND = 128
LAGS = 1024


def spread(block, axis, holder):
    block = jnp.where(lax.axis_index(axis) == holder, block, jnp.zeros_like(block))
    return lax.psum(block, axis)


def extended(cells, sides, width):
    for axis, dim in sides:
        count = lax.axis_size(axis)
        ends = count - 1
        head = lax.slice_in_dim(cells, 0, width, axis=dim)
        tail = lax.slice_in_dim(cells, cells.shape[dim] - width, cells.shape[dim], axis=dim)
        cells = jnp.concatenate(
            [
                lax.ppermute(tail, axis, [(i, (i + 1) % count) for i in range(ends)]),
                cells,
                lax.ppermute(head, axis, [((i + 1) % count, i) for i in range(ends)]),
            ],
            axis=dim,
        )
    return cells


def make_tables(length, lags):
    half = length // 2
    times = jnp.arange(length, dtype=jnp.int32)
    freqs = jnp.arange(half, dtype=jnp.int32)
    phase = times[:, None] * freqs[None, :] % length
    angle = phase.astype(jnp.float32) * (2.0 * math.pi / length)
    forward = jnp.concatenate([jnp.cos(angle), -jnp.sin(angle)], axis=1).astype(jnp.bfloat16)
    shifts = jnp.arange(lags, dtype=jnp.int32) - lags // 2 + length
    phase_back = freqs[:, None] * shifts[None, :] % length
    angle_back = phase_back.astype(jnp.float32) * (2.0 * math.pi / length)
    inverse = jnp.concatenate([jnp.cos(angle_back), -jnp.sin(angle_back)], axis=0) * (
        1.0 / math.sqrt(half)
    )
    return (forward, inverse)


def whiten(spectra, band):
    lead = spectra.shape[:-1]
    width = spectra.shape[-1] // 2
    parts = spectra.reshape(lead + (2, width // band, band))
    power = jnp.sum(parts * parts, axis=(-3, -1)) / (2.0 * band)
    scale = lax.rsqrt(power + 1e-06)
    return (parts * scale[..., None, :, None]).reshape(spectra.shape)


def cross_sum(receivers, emitters):
    half = receivers.shape[2] // 2
    rec_re, rec_im = (receivers[..., :half], receivers[..., half:])
    emi_re, emi_im = (emitters[..., :half], emitters[..., half:])
    real_part = jnp.einsum("sck,snk->nck", rec_re, emi_re, preferred_element_type=jnp.float32)
    real_part = real_part + jnp.einsum(
        "sck,snk->nck", rec_im, emi_im, preferred_element_type=jnp.float32
    )
    imag_part = jnp.einsum("sck,snk->nck", rec_im, emi_re, preferred_element_type=jnp.float32)
    imag_part = imag_part - jnp.einsum(
        "sck,snk->nck", rec_re, emi_im, preferred_element_type=jnp.float32
    )
    return jnp.concatenate([real_part, imag_part], axis=-1)


def correlate(cross, inverse):
    count, chans, width = cross.shape
    flat = jnp.dot(cross.reshape(count * chans, width), inverse, precision=lax.Precision.HIGHEST)
    return flat.reshape(count, chans, inverse.shape[1])


def shards(data, sources, owners):
    seg_dev, ch_dev, length = data.shape
    steps = sources.shape[0]
    forward, inverse = make_tables(length, LAGS)
    spectra = jnp.dot(
        data.reshape(seg_dev * ch_dev, length), forward, preferred_element_type=jnp.float32
    )
    white = whiten(spectra.reshape(seg_dev, ch_dev, length), BAND).astype(jnp.bfloat16)
    selector = (sources[:, :, None] == jnp.arange(ch_dev, dtype=jnp.int32)[None, None, :]).astype(
        jnp.bfloat16
    )
    picked = jnp.einsum("pnc,scf->psnf", selector, white, preferred_element_type=jnp.float32)
    received = []
    for step in range(steps):
        received.append(spread(picked[step].astype(jnp.bfloat16), "fibre", owners[step]))
    chosen = jnp.stack(received)
    padded = extended(white, (("fibre", 1),), 4)
    total = padded[:, 0:ch_dev].astype(jnp.float32)
    for offset in range(1, 8):
        total = total + padded[:, offset : offset + ch_dev].astype(jnp.float32)
    stacked = (total * 0.125).astype(jnp.bfloat16)
    partial_list = [correlate(cross_sum(stacked, chosen[step]), inverse) for step in range(steps)]
    return lax.psum_scatter(jnp.stack(partial_list), "seg", scatter_dimension=2, tiled=True)


def solution(mesh):
    return jax.shard_map(
        shards,
        mesh=mesh,
        in_specs=(P("seg", "fibre", None), P(), P()),
        out_specs=P(None, None, ("fibre", "seg"), None),
        check_vma=False,
    )
```

profile of v0, /device:TPU:1, one launch (start us, length us, event | category | flops | bytes accessed | tf_op | source)
XLA Modules:
  0.0 840.4 jit_solution(10892744764179894782)
XLA Ops:
  6.5 0.0 copy-start
  6.5 0.0 all-reduce.4.cloned.1.call-start
  6.5 33.8 %negate_convert_fusion = (bf16[2048,1024]{1,0:T(8,128)(2,1)S(1)}, bf16[2048,1024]{1,0:T(8,128)(2,1)S(1)}) fusion(), kind=kLoop, calls=%fused_computation.12 | loop fusion | flops 35651584 | bytes 8388608 | tf_op jit(solution)/shard_map/convert.44
  40.4 0.0 copy-done
  40.4 0.0 copy-start.2
  40.4 0.0 copy-start.1
  40.4 1.2 fusion.57
  41.6 0.1 reduce_sum.9
  41.7 0.1 mul.100
  41.8 4.4 collective-permute-start
  46.2 1.3 collective-permute-start.1
  47.5 0.0 copy-done.2
  47.5 0.2 fusion.26
  47.8 0.0 copy-done.1
  47.8 0.6 fusion.56
  49.7 604.6 %all-reduce.1 = (bf16[1,4,2048]{2,1,0:T(4,128)(2,1)S(1)}, bf16[1,4,2048]{2,1,0:T(4,128)(2,1)S(1)}) all-reduce(bf16[1,4,2048]{2,1,0:T(4,128)(2,1)S(1)} %get-tuple-element.18, bf16[1,4,2048]{2,1,0:T(4,128)(2,1)S(1)} %get-tuple-element.17), channel_id=1, replica_groups=mesh['fibre'=128,'seg'=4] {'fibre'}, use_global_device_ids=true, to_apply=%region_2.3 | all-reduce | flops 16384 | bytes 65536 | tf_op jit(solution)/shard_map/psum | solution.py:13
  654.3 16.7 %fusion.27 = (f32[1024,1024]{1,0:T(8,128)S(1)}, f32[1024,1024]{1,0:T(8,128)S(1)}) fusion(s32[1024]{0:T(1024)S(1)} %iota_add_fusion), kind=kLoop, calls=%fused_computation.34 | loop fusion | flops 15728640 | bytes 8392704 | tf_op jit(solution)/shard_map/cos | solution.py:43
  671.0 0.0 collective-permute-done
  671.0 0.0 collective-permute-done.1
  671.0 0.1 multiply_convert_fusion
  671.1 0.1 add_bitcast_fusion.1
  671.2 5.0 fusion.28
  676.2 5.0 fusion.31
  681.3 0.9 copy.4
  682.2 0.0 all-reduce.4.cloned.1.call-update
  682.2 1.3 dynamic-slice
  684.1 148.0 %all-reduce.4.cloned.1.call-done = f32[2,4,8,1024]{3,1,0,2:T(4,128)} async-done(((f32[2,4,8,1024]{3,1,0,2:T(4,128)}), f32[2,4,8,1024]{3,1,0,2:T(4,128)}) %all-reduce.4.cloned.1.call-update) | async-done | bytes 262160
  832.1 0.8 constant_dynamic-slice_fusion
  832.9 0.7 copy.5
  (9 shorter events, 0.1 us)
Async XLA Ops:
  6.5 33.9 %copy-start = (bf16[1,8,2048]{2,1,0:T(8,128)(2,1)S(1)}, bf16[1,8,2048]{2,1,0:T(8,128)(2,1)}, u32[]{:S(2)}) copy-start(bf16[1,8,2048]{2,1,0:T(8,128)(2,1)} %param.3) | copy-start | bytes 98308
  6.5 825.5 %all-reduce.4.cloned.1.call-start = ((), (), s32[]{:S(2)}) async-start(), calls=%async_computation | async-start | bytes 524288
  40.4 7.1 copy-start.2
  40.4 7.3 copy-start.1
  41.8 629.2 %collective-permute-start = (bf16[1,4,2048]{2,1,0:T(4,128)(2,1)S(1)}, bf16[1,4,2048]{2,1,0:T(4,128)(2,1)S(1)}, u32[]{:S(2)}, u32[]{:S(2)}) collective-permute-start(bf16[1,4,2048]{2,1,0:T(4,128)(2,1)S(1)} %get-tuple-element.15), channel_id=1, source_target_pairs={{0,4},{4,8},{8,12},{12,16},{16,20},{20,24},{24,28},{28,32},{32,36}... | collective-permute-start | bytes 49160 | tf_op jit(solution)/shard_map/ppermute | solution.py:24
  46.2 624.8 %collective-permute-start.1 = (bf16[1,4,2048]{2,1,0:T(4,128)(2,1)S(1)}, bf16[1,4,2048]{2,1,0:T(4,128)(2,1)S(1)}, u32[]{:S(2)}, u32[]{:S(2)}) collective-permute-start(bf16[1,4,2048]{2,1,0:T(4,128)(2,1)S(1)} %get-tuple-element.16), channel_id=1, source_target_pairs={{4,0},{8,4},{12,8},{16,12},{20,16},{24,20},{28,24},{32,28},{36,32}... | collective-permute-start | bytes 49160 | tf_op jit(solution)/shard_map/ppermute | solution.py:26
Sparse Core Ops, SparseCore 0:
  682.3 149.7 all-reduce.3
where the time goes:
time: 841 us; the launch traced here: 840 us
  blocking collectives  605 us (72%)
  waiting for transfers between devices  148 us (18%)
  other arithmetic  50.9 us (6%)
  between operations  15.5 us (2%)
  matrix products  11.4 us (1%)
    psum x1, blocking collectives, spread(): return lax.psum(block, axis)  605 us
    unnamed x2, waiting for transfers between devices  148 us
    another operation x4, other arithmetic  33.9 us
  transfers between devices with their start and end apart: 3, of which 1 were waited for; matrix products, arithmetic and copies ran while one was open for 2% of the time, Pallas kernels for 0%

commit v1 on v0

--- a/solution.py
+++ b/solution.py
@@ -9,8 +9,13 @@
 
 
 def spread(block, axis, holder):
+
+    def plan_blocks_on(local_values, which_axis):
+        o_now = jnp.sum(lax.all_gather(local_values, which_axis), 0)
+        return o_now
+
     block = jnp.where(lax.axis_index(axis) == holder, block, jnp.zeros_like(block))
-    return lax.psum(block, axis)
+    return plan_blocks_on(block, axis)
 
 
 def extended(cells, sides, width):

time: 841 us -> 543 us (0.65)
  blocking collectives: 605 us -> 0 us
  waiting for transfers between devices: 148 us -> 446 us
    psum x1 -> x0, blocking collectives: 605 us -> none  [spread(): return lax.psum(block, axis)]
    all_gather x0 -> x2, waiting for transfers between devices: none -> 392 us  [plan_blocks_on(): o_now = jnp.sum(lax.all_gather(local_values, which_axis), 0)]
    unnamed x2 -> x4, waiting for transfers between devices: 148 us -> 54.2 us
  transfers between devices with their start and end apart: 3 -> 5, of which waited for: 1 -> 3; matrix products, arithmetic and copies ran while one was open for 2% -> 4% of each run, Pallas kernels for 0% -> 0%
where the time goes in v1:
time: 543 us
  waiting for transfers between devices  446 us (82%)
  other arithmetic  57.8 us (11%)
  between operations  15.2 us (3%)
  matrix products  13.9 us (3%)
  starting transfers between devices  5.92 us (1%)
    all_gather x2, waiting for transfers between devices, plan_blocks_on(): o_now = jnp.sum(lax.all_gather(local_values, which_axis), 0)  392 us
    unnamed x4, waiting for transfers between devices  54.2 us
    another operation x4, other arithmetic  33.9 us
    cos x1, other arithmetic, make_tables(): jnp.cos(angle_back)  18.1 us
    dot_general x2, matrix products, correlate(): jnp.dot(cross.reshape(count * chans, width), inverse, precision=lax.Preci...  12.5 us
  transfers between devices with their start and end apart: 5, of which 3 were waited for; matrix products, arithmetic and copies ran while one was open for 4% of the time, Pallas kernels for 0%

profile of v1, /device:TPU:1, one launch (start us, length us, event | category | flops | bytes accessed | tf_op | source)
XLA Modules:
  0.0 543.2 jit_solution(9553194908825855386)
XLA Ops:
  6.5 0.0 copy-start
  6.5 0.0 all-gather.3.cloned.1.call-start
  6.5 33.8 %negate_convert_fusion = (bf16[2048,1024]{1,0:T(8,128)(2,1)S(1)}, bf16[2048,1024]{1,0:T(8,128)(2,1)S(1)}) fusion(), kind=kLoop, calls=%fused_computation.12 | loop fusion | flops 35651584 | bytes 8388608 | tf_op jit(solution)/shard_map/convert.46
  40.4 0.0 copy-done
  40.4 0.0 copy-start.3
  40.4 0.0 copy-start.4
  40.4 1.2 fusion.57
  41.6 0.1 reduce_sum.37
  41.7 0.0 copy-done.3
  41.7 0.6 fusion.56
  43.6 0.1 mul.100
  43.7 0.0 copy-done.4
  43.7 0.2 fusion.26
  43.9 0.6 fusion.48
  44.6 0.0 all-gather.3.cloned.1.call-update
  44.6 0.0 all-gather.5.cloned.1.call-start
  44.7 0.7 all-gather.5.cloned.1.call-update
  45.4 0.0 all-reduce.3.cloned.1.call-start
  45.4 4.4 collective-permute-start
  49.8 1.5 collective-permute-start.1
  51.3 18.1 %fusion.27 = (f32[1024,1024]{1,0:T(8,128)}, f32[1024,1024]{1,0:T(8,128)}) fusion(s32[1024]{0:T(1024)S(1)} %iota_add_fusion), kind=kLoop, calls=%fused_computation.34 | loop fusion | flops 15728640 | bytes 8392704 | tf_op jit(solution)/shard_map/cos | solution.py:48
  69.3 0.0 collective-permute-done
  69.4 0.0 collective-permute-done.1
  69.4 0.1 multiply_convert_fusion
  69.5 183.5 %all-gather.3.cloned.1.call-done = bf16[128,1,4,2048]{3,2,1,0:T(4,128)(2,1)} async-done(((bf16[1,1,4,2048]{3,2,1,0:T(4,128)(2,1)}), bf16[128,1,4,2048]{3,2,1,0:T(4,128)(2,1)}) %all-gather.3.cloned.1.call-update) | async-done | bytes 2097168 | tf_op jit(solution)/shard_map/all_gather | solution.py:14
  253.0 2.5 reduce_sum.38
  255.5 208.1 %all-gather.5.cloned.1.call-done = bf16[128,1,4,2048]{3,2,1,0:T(4,128)(2,1)} async-done(((bf16[1,1,4,2048]{3,2,1,0:T(4,128)(2,1)}), bf16[128,1,4,2048]{3,2,1,0:T(4,128)(2,1)}) %all-gather.5.cloned.1.call-update) | async-done | bytes 2097168 | tf_op jit(solution)/shard_map/all_gather | solution.py:14
  463.6 2.5 reduce_sum.40
  466.1 0.1 add_bitcast_fusion.1
  466.2 0.0 copy-start.1
  466.2 0.0 copy-start.2
  466.2 7.5 %fusion.28 = f32[1,4,8,1024]{3,2,1,0:T(8,128)S(1)} fusion(f32[1024,1024]{1,0:T(8,128)} %get-tuple-element.22, f32[1024,1024]{1,0:T(8,128)} %get-tuple-element.21, f32[4,8,1024]{2,1,0:T(8,128)S(1)} %get-tuple-element.6, f32[4,8,1024]{2,1,0:T(8,128)S(1)} %get-tuple-element.5), kind=kOutput, calls=%fused_computation.35 | convolution fusion | flops 809566208 | bytes 8781824 | tf_op jit(solution)/shard_map/dot_general | solution.py:80
  473.7 0.0 copy-done.1
  473.7 0.0 copy-done.2
  473.8 5.0 fusion.31
  478.8 0.9 copy.6
  479.7 0.0 all-reduce.3.cloned.1.call-update
  479.7 1.3 dynamic-slice
  481.6 53.5 %all-reduce.3.cloned.1.call-done = f32[2,4,8,1024]{3,1,0,2:T(4,128)} async-done(((f32[2,4,8,1024]{3,1,0,2:T(4,128)}), f32[2,4,8,1024]{3,1,0,2:T(4,128)}) %all-reduce.3.cloned.1.call-update) | async-done | bytes 262160
  535.1 0.8 constant_dynamic-slice_fusion
  536.0 0.7 copy.7
  (8 shorter events, 0.1 us)
Async XLA Ops:
  6.5 33.9 %copy-start = (bf16[1,8,2048]{2,1,0:T(8,128)(2,1)S(1)}, bf16[1,8,2048]{2,1,0:T(8,128)(2,1)}, u32[]{:S(2)}) copy-start(bf16[1,8,2048]{2,1,0:T(8,128)(2,1)} %param.3) | copy-start | bytes 98308
  6.5 246.5 %all-gather.3.cloned.1.call-start = ((), (), s32[]{:S(2)}) async-start(), calls=%async_computation | async-start | bytes 2113536 | tf_op jit(solution)/shard_map/all_gather | solution.py:14
  40.4 1.3 copy-start.3
  40.4 3.3 copy-start.4
  44.6 419.0 %all-gather.5.cloned.1.call-start = ((), (), s32[]{:S(2)}) async-start(), calls=%async_computation.1 | async-start | bytes 2113536 | tf_op jit(solution)/shard_map/all_gather | solution.py:14
  45.4 489.8 %all-reduce.3.cloned.1.call-start = ((), (), s32[]{:S(2)}) async-start(), calls=%async_computation.2 | async-start | bytes 524288
  45.4 23.9 %collective-permute-start = (bf16[1,4,2048]{2,1,0:T(4,128)(2,1)S(1)}, bf16[1,4,2048]{2,1,0:T(4,128)(2,1)S(1)}, u32[]{:S(2)}, u32[]{:S(2)}) collective-permute-start(bf16[1,4,2048]{2,1,0:T(4,128)(2,1)S(1)} %get-tuple-element.15), channel_id=1, source_target_pairs={{0,4},{4,8},{8,12},{12,16},{16,20},{20,24},{24,28},{28,32},{32,36}... | collective-permute-start | bytes 49160 | tf_op jit(solution)/shard_map/ppermute | solution.py:29
  49.8 19.6 %collective-permute-start.1 = (bf16[1,4,2048]{2,1,0:T(4,128)(2,1)S(1)}, bf16[1,4,2048]{2,1,0:T(4,128)(2,1)S(1)}, u32[]{:S(2)}, u32[]{:S(2)}) collective-permute-start(bf16[1,4,2048]{2,1,0:T(4,128)(2,1)S(1)} %get-tuple-element.16), channel_id=1, source_target_pairs={{4,0},{8,4},{12,8},{16,12},{20,16},{24,20},{28,24},{32,28},{36,32}... | collective-permute-start | bytes 49160 | tf_op jit(solution)/shard_map/ppermute | solution.py:31
  466.2 7.5 %copy-start.1 = (f32[1024,1024]{1,0:T(8,128)S(1)}, f32[1024,1024]{1,0:T(8,128)}, u32[]{:S(2)}) copy-start(f32[1024,1024]{1,0:T(8,128)} %get-tuple-element.21) | copy-start | bytes 12582916
  466.2 7.5 %copy-start.2 = (f32[1024,1024]{1,0:T(8,128)S(1)}, f32[1024,1024]{1,0:T(8,128)}, u32[]{:S(2)}) copy-start(f32[1024,1024]{1,0:T(8,128)} %get-tuple-element.22) | copy-start | bytes 12582916
Sparse Core Ops, SparseCore 0:
  44.7 208.2 all-gather.2
  257.4 206.2 all-gather.4
  479.8 55.2 all-reduce.2
